TPU v7x, 512 devices: a whole 4x8x8 slice. The times are simulated.
512 devices in a mesh: shot: 32 (over z, y_hi), dom: 16 (over x, y_lo, core).
Axes of the slice: x: 4, y: 8 (y_hi: 4, y_lo: 2; y = y_hi * 2 + y_lo), z: 8, core: 2. Of those that a mesh axis runs over, the one named last changes fastest.
Arguments:
- coefficient: float32 [512, 16, 384], P('dom'), may hold values from 0.02 to 0.18
- fwd_older: float32 [32, 512, 16, 384], P('shot', 'dom'), may hold values from -6 to 6
- fwd_recent: float32 [32, 512, 16, 384], P('shot', 'dom'), may hold values from -6 to 6
- adj_later: float32 [32, 512, 16, 384], P('shot', 'dom'), may hold values from -6 to 6
- adj_recent: float32 [32, 512, 16, 384], P('shot', 'dom'), may hold values from -6 to 6
- source_xcell: int32 [32], P('shot'), may hold values from 0 to 511
- source_ycell: int32 [32], P('shot'), may hold values from 0 to 15
- source_zcell: int32 [32], P('shot'), may hold values from 0 to 383
- amplitude: float32 [32, 2], P('shot'), may hold values from 3547.24 to 7094.48
- receiver_xcell: int32 [32, 1024], P('shot'), may hold values from 0 to 511
- receiver_ycell: int32 [32, 1024], P('shot'), may hold values from 0 to 15
- receiver_zcell: int32 [32, 1024], P('shot'), may hold values from 0 to 383
- observed: float32 [32, 2, 1024], P('shot'), may hold values from -6 to 6
Outputs:
- fwd_latest: float32 [32, 512, 16, 384], P('shot', 'dom')
- adj_latest: float32 [32, 512, 16, 384], P('shot', 'dom')
- model_gradient: float32 [512, 16, 384], P('dom')
All inputs are finite; a program needn't handle non-finite values.
Results may differ from a plain program's by a relative error of at most 0.0003.
Values sent between devices are 32-bit elements; how exact they have to be, the bound alone decides.
No kernel may reach another device: no remote copies, remote signals or barrier semaphores. Data moves between devices by JAX's collectives and lax.ppermute only.
A program may use at most 64 MiB of HBM per device.

v0:
```python
import jax
import jax.numpy as jnp
from jax import lax
from jax.sharding import PartitionSpec as P

R = 4
stencil_weights = (-205.0 / 72.0, 8.0 / 5.0, -1.0 / 5.0, 8.0 / 315.0, -1.0 / 560.0)


def with_halo(block, sides, width):
    for axis, dim in sides:
        count = lax.axis_size(axis)
        forward = [(i, i + 1) for i in range(count - 1)]
        backward = [(target, source) for source, target in forward]
        low = lax.ppermute(
            lax.slice_in_dim(block, block.shape[dim] - width, None, axis=dim), axis, forward
        )
        high = lax.ppermute(lax.slice_in_dim(block, 0, width, axis=dim), axis, backward)
        block = jnp.concatenate([low, block, high], axis=dim)
    return block


def laplace_core(extended):
    count = extended.shape[0] - 2 * R
    center = extended[R : R + count]
    width_y = center.shape[1]
    width_z = center.shape[2]
    total = 3.0 * stencil_weights[0] * center
    padded = jnp.pad(center, ((0, 0), (R, R), (R, R)))
    for offset in range(1, R + 1):
        weight = stencil_weights[offset]
        total = total + weight * (
            extended[R + offset : R + offset + count] + extended[R - offset : R - offset + count]
        )
        total = total + weight * (
            padded[:, R + offset : R + offset + width_y, R : R + width_z]
            + padded[:, R - offset : R - offset + width_y, R : R + width_z]
        )
        total = total + weight * (
            padded[:, R : R + width_y, R + offset : R + offset + width_z]
            + padded[:, R : R + width_y, R - offset : R - offset + width_z]
        )
    return total


def point_grid(shape, xcells, ycells, zcells, values, start):
    count = shape[0]
    inside = (xcells >= start) & (xcells < start + count)
    local = jnp.clip(xcells - start, 0, count - 1)
    kept = jnp.where(inside, values, jnp.zeros_like(values))
    return jnp.zeros(shape, values.dtype).at[local, ycells, zcells].add(kept)


def sample(field, xcells, ycells, zcells, start):
    count = field.shape[0]
    inside = (xcells >= start) & (xcells < start + count)
    local = jnp.clip(xcells - start, 0, count - 1)
    picked = field[local, ycells, zcells]
    return jnp.where(inside, picked, jnp.zeros_like(picked))


def shards(
    coefficient,
    fwd_older,
    fwd_recent,
    adj_later,
    adj_recent,
    source_xcell,
    source_ycell,
    source_zcell,
    amplitude,
    receiver_xcell,
    receiver_ycell,
    receiver_zcell,
    observed,
):
    count = coefficient.shape[0]
    shape = coefficient.shape
    base = lax.axis_index("dom") * count
    older = fwd_older[0]
    recent = fwd_recent[0]
    later = adj_later[0]
    adj_now = adj_recent[0]
    rxc = receiver_xcell[0]
    ryc = receiver_ycell[0]
    rzc = receiver_zcell[0]

    def advance(current, before, sources):
        extended = with_halo(current, (("dom", 0),), R)
        return 2.0 * current - before + coefficient * (laplace_core(extended) + sources)

    fwd_two = advance(
        recent,
        older,
        point_grid(shape, source_xcell, source_ycell, source_zcell, amplitude[0, 0:1], base),
    )
    fwd_three = advance(
        fwd_two,
        recent,
        point_grid(shape, source_xcell, source_ycell, source_zcell, amplitude[0, 1:2], base),
    )
    samples = jnp.stack(
        [sample(fwd_two, rxc, ryc, rzc, base), sample(fwd_three, rxc, ryc, rzc, base)]
    )
    traces = lax.psum(samples, "dom")
    resid_two = traces[0] - observed[0, 0]
    resid_three = traces[1] - observed[0, 1]
    adj_two = advance(adj_now, later, point_grid(shape, rxc, ryc, rzc, resid_three, base))
    late_term = adj_two * (fwd_three - 2.0 * fwd_two + recent)
    adj_one = advance(adj_two, adj_now, point_grid(shape, rxc, ryc, rzc, resid_two, base))
    early_term = adj_one * (fwd_two - 2.0 * recent + older)
    gradient = lax.psum(early_term + late_term, "shot")
    return (fwd_three[None], adj_one[None], gradient)


def solution(mesh):
    return jax.shard_map(
        shards,
        mesh=mesh,
        in_specs=(
            P("dom", None, None),
            P("shot", "dom", None, None),
            P("shot", "dom", None, None),
            P("shot", "dom", None, None),
            P("shot", "dom", None, None),
            P("shot"),
            P("shot"),
            P("shot"),
            P("shot", None),
            P("shot", None),
            P("shot", None),
            P("shot", None),
            P("shot", None, None),
        ),
        out_specs=(
            P("shot", "dom", None, None),
            P("shot", "dom", None, None),
            P("dom", None, None),
        ),
        check_vma=False,
    )
```

profile of v0, /device:TPU:2, one launch (start us, length us, event | category | flops | bytes accessed | tf_op | source)
XLA Modules:
  0.0 466.0 jit_solution(8528080193020406598)
XLA Ops:
  7.3 1.7 slice_bitcast_fusion.1
  9.0 2.9 collective-permute-start.4
  11.9 1.9 collective-permute-start.5
  14.8 4.5 collective-permute-start
  19.3 1.9 collective-permute-start.1
  28.6 2.7 fusion.80
  34.9 4.5 collective-permute-start.2
  39.4 1.9 collective-permute-start.3
  41.4 2.7 fusion.32
  44.1 10.6 %gather_fusion = f32[1024]{0:T(1024)S(1)} fusion(f32[32,16,384]{2,1,0:T(8,128)S(1)} %fusion.169, s32[1024]{0:T(1024)S(1)} %bitcast.63), kind=kCustom, calls=%fused_computation | custom fusion | bytes 20480 | tf_op jit(solution)/shard_map/gather | solution.py:58
  54.8 3.5 fusion.56
  61.6 1.6 multiply_add_fusion.1
  63.2 10.6 %gather_fusion.1 = f32[1024]{0:T(1024)S(1)} fusion(f32[32,16,384]{2,1,0:T(8,128)S(1)} %multiply_add_fusion.1, s32[1024]{0:T(1024)S(1)} %bitcast.64), kind=kCustom, calls=%fused_computation.1 | custom fusion | bytes 20480 | tf_op jit(solution)/shard_map/gather | solution.py:58
  73.8 25.4 %psum.14 = f32[2,1024]{1,0:T(2,128)S(1)} all-reduce(f32[2,1024]{1,0:T(2,128)S(1)} %pad_maximum_fusion.8), channel_id=1, replica_groups=mesh['shot'=32,'dom'=16] {'dom'}, use_global_device_ids=true, to_apply=%region_1.2 | all-reduce | flops 2048 | bytes 16384 | tf_op jit(solution)/shard_map/psum | solution.py:105
  99.3 6.4 %scatter_fusion = f32[196608]{0:T(1024)S(1)} fusion(f32[196608]{0:T(1024)S(1)} %reshape.178, s32[1024]{0:T(1024)S(1)} %broadcast_select_fusion, f32[1024]{0:T(1024)S(1)} %get-tuple-element.48), kind=kCustom, calls=%fused_computation.2 | custom fusion | flops 1024 | bytes 16384
  106.7 2.0 fusion.168
  108.8 2.5 collective-permute-start.6
  111.3 1.9 collective-permute-start.7
  113.5 5.5 %collective-permute-done.7 = f32[4,16,384]{2,1,0:T(8,128)S(1)} collective-permute-done((f32[4,16,384]{2,1,0:T(8,128)S(1)}, f32[4,16,384]{2,1,0:T(8,128)S(1)}, u32[]{:S(2)}, u32[]{:S(2)}) %collective-permute-start.7) | collective-permute-done | bytes 98336 | tf_op jit(solution)/shard_map/ppermute | solution.py:15
  119.0 3.5 fusion.8
  123.7 6.4 %scatter_fusion.1 = f32[196608]{0:T(1024)S(1)} fusion(f32[196608]{0:T(1024)S(1)} %reshape.182, s32[1024]{0:T(1024)S(1)} %broadcast_select_fusion, f32[1024]{0:T(1024)S(1)} %get-tuple-element.47), kind=kCustom, calls=%fused_computation.3 | custom fusion | flops 1024 | bytes 16384
  131.1 3.6 fusion.171
  134.7 322.4 %all-reduce.6.cloned.1.call-done = f32[32,16,384]{2,1,0:T(8,128)} async-done(((f32[32,16,384]{2,1,0:T(8,128)}), f32[32,16,384]{2,1,0:T(8,128)}) %all-reduce.6.cloned.1.call-update) | async-done | bytes 786448 | tf_op jit(solution)/shard_map/psum | solution.py:112
  457.1 2.1 copy.24
  (63 shorter events, 13.0 us)
Async XLA Ops:
  7.2 18.0 %copy-start.14 = (s32[3]{0:T(128)S(1)}, s32[3]{0:T(128)}, u32[]{:S(2)}) copy-start(s32[3]{0:T(128)} %constant.78.clone.1) | copy-start | bytes 40
  7.2 20.6 %copy-start.12 = (s32[3]{0:T(128)S(1)}, s32[3]{0:T(128)}, u32[]{:S(2)}) copy-start(s32[3]{0:T(128)} %constant.108) | copy-start | bytes 40
  7.2 20.7 %copy-start.13 = (s32[3]{0:T(128)S(1)}, s32[3]{0:T(128)}, u32[]{:S(2)}) copy-start(s32[3]{0:T(128)} %constant.105) | copy-start | bytes 40
  7.2 21.4 %copy-start.1 = (f32[1,32,16,384]{3,2,1,0:T(8,128)S(1)}, f32[1,32,16,384]{3,2,1,0:T(8,128)}, u32[]{:S(2)}) copy-start(f32[1,32,16,384]{3,2,1,0:T(8,128)} %param.19) | copy-start | bytes 2359300
  7.2 16.0 %copy-start.11 = (f32[1,2]{1,0:T(1,128)S(1)}, f32[1,2]{1,0:T(1,128)}, u32[]{:S(2)}) copy-start(f32[1,2]{1,0:T(1,128)} %param.25) | copy-start | bytes 28
  7.2 19.9 %copy-start.7 = (f32[1,2,1024]{2,1,0:T(2,128)S(1)}, f32[1,2,1024]{2,1,0:T(2,128)}, u32[]{:S(2)}) copy-start(f32[1,2,1024]{2,1,0:T(2,128)} %param.29) | copy-start | bytes 24580
  7.2 20.5 %copy-start.5 = (s32[1,1024]{1,0:T(1,128)S(1)}, s32[1,1024]{1,0:T(1,128)}, u32[]{:S(2)}) copy-start(s32[1,1024]{1,0:T(1,128)} %param.26) | copy-start | bytes 12292
  7.2 20.5 %copy-start.9 = (s32[1,1024]{1,0:T(1,128)S(1)}, s32[1,1024]{1,0:T(1,128)}, u32[]{:S(2)}) copy-start(s32[1,1024]{1,0:T(1,128)} %param.28) | copy-start | bytes 12292
  7.3 20.5 %copy-start.8 = (s32[1,1024]{1,0:T(1,128)S(1)}, s32[1,1024]{1,0:T(1,128)}, u32[]{:S(2)}) copy-start(s32[1,1024]{1,0:T(1,128)} %param.27) | copy-start | bytes 12292
  7.3 449.8 %all-reduce.6.cloned.1.call-start = ((), (), s32[]{:S(2)}) async-start(), calls=%async_computation | async-start | bytes 1572864 | tf_op jit(solution)/shard_map/psum | solution.py:112
  9.0 32.4 %collective-permute-start.4 = (f32[4,16,384]{2,1,0:T(8,128)}, f32[4,16,384]{2,1,0:T(8,128)S(1)}, u32[]{:S(2)}, u32[]{:S(2)}) collective-permute-start(f32[4,16,384]{2,1,0:T(8,128)} %get-tuple-element.33), channel_id=1, source_target_pairs={{1,0},{2,1},{3,2},{4,3},{5,4},{6,5},{7,6},{8,7},{9,8},{10,9},{11,1... | collective-permute-start | bytes 294920 | tf_op jit(solution)/shard_map/ppermute | solution.py:18
  11.9 29.5 %collective-permute-start.5 = (f32[4,16,384]{2,1,0:T(8,128)}, f32[4,16,384]{2,1,0:T(8,128)S(1)}, u32[]{:S(2)}, u32[]{:S(2)}) collective-permute-start(f32[4,16,384]{2,1,0:T(8,128)} %get-tuple-element.34), channel_id=1, source_target_pairs={{0,1},{1,2},{2,3},{3,4},{4,5},{5,6},{6,7},{7,8},{8,9},{9,10},{10,1... | collective-permute-start | bytes 294920 | tf_op jit(solution)/shard_map/ppermute | solution.py:15
  14.8 13.9 %collective-permute-start = (f32[4,16,384]{2,1,0:T(8,128)S(1)}, f32[4,16,384]{2,1,0:T(8,128)S(1)}, u32[]{:S(2)}, u32[]{:S(2)}) collective-permute-start(f32[4,16,384]{2,1,0:T(8,128)S(1)} %get-tuple-element.37), channel_id=1, source_target_pairs={{1,0},{2,1},{3,2},{4,3},{5,4},{6,5},{7,6},{8,7},{9,8},{10,9},{11,1... | collective-permute-start | bytes 294920 | tf_op jit(solution)/shard_map/ppermute | solution.py:18
  19.3 9.3 %collective-permute-start.1 = (f32[4,16,384]{2,1,0:T(8,128)S(1)}, f32[4,16,384]{2,1,0:T(8,128)S(1)}, u32[]{:S(2)}, u32[]{:S(2)}) collective-permute-start(f32[4,16,384]{2,1,0:T(8,128)S(1)} %get-tuple-element.38), channel_id=1, source_target_pairs={{0,1},{1,2},{2,3},{3,4},{4,5},{5,6},{6,7},{7,8},{8,9},{9,10},{10,1... | collective-permute-start | bytes 294920 | tf_op jit(solution)/shard_map/ppermute | solution.py:15
  28.6 4.1 copy-start.2
  32.8 8.6 %copy-start.3 = (f32[1,32,16,384]{3,2,1,0:T(8,128)S(1)}, f32[1,32,16,384]{3,2,1,0:T(8,128)}, u32[]{:S(2)}) copy-start(f32[1,32,16,384]{3,2,1,0:T(8,128)} %param.21) | copy-start | bytes 2359300
  34.9 19.9 %collective-permute-start.2 = (f32[4,16,384]{2,1,0:T(8,128)}, f32[4,16,384]{2,1,0:T(8,128)S(1)}, u32[]{:S(2)}, u32[]{:S(2)}) collective-permute-start(f32[4,16,384]{2,1,0:T(8,128)} %get-tuple-element.35), channel_id=1, source_target_pairs={{1,0},{2,1},{3,2},{4,3},{5,4},{6,5},{7,6},{8,7},{9,8},{10,9},{11,1... | collective-permute-start | bytes 294920 | tf_op jit(solution)/shard_map/ppermute | solution.py:18
  39.4 15.3 %collective-permute-start.3 = (f32[4,16,384]{2,1,0:T(8,128)}, f32[4,16,384]{2,1,0:T(8,128)S(1)}, u32[]{:S(2)}, u32[]{:S(2)}) collective-permute-start(f32[4,16,384]{2,1,0:T(8,128)} %get-tuple-element.36), channel_id=1, source_target_pairs={{0,1},{1,2},{2,3},{3,4},{4,5},{5,6},{6,7},{7,8},{8,9},{9,10},{10,1... | collective-permute-start | bytes 294920 | tf_op jit(solution)/shard_map/ppermute | solution.py:15
  63.1 68.0 %copy-start = (f32[32,16,384]{2,1,0:T(8,128)}, f32[32,16,384]{2,1,0:T(8,128)S(1)}, u32[]{:S(2)}) copy-start(f32[32,16,384]{2,1,0:T(8,128)S(1)} %multiply_add_fusion.1) | copy-start | bytes 2359300
  63.1 36.1 %copy-start.6 = (f32[1,1,1024]{2,1,0:T(1,128)S(1)}, f32[1,1,1024]{2,1,0:T(1,128)}, u32[]{:S(2)}) copy-start(f32[1,1,1024]{2,1,0:T(1,128)} %get-tuple-element.40) | copy-start | bytes 12292
  63.2 36.1 %copy-start.10 = (pred[1024]{0:T(1024)(128)(4,1)S(1)}, pred[1024]{0:T(1024)(128)(4,1)}, u32[]{:S(2)}) copy-start(pred[1024]{0:T(1024)(128)(4,1)} %fusion.172) | copy-start | bytes 3076
  108.7 10.3 %copy-start.4 = (f32[32,16,384]{2,1,0:T(8,128)}, f32[32,16,384]{2,1,0:T(8,128)S(1)}, u32[]{:S(2)}) copy-start(f32[32,16,384]{2,1,0:T(8,128)S(1)} %fusion.168) | copy-start | bytes 2359300
  108.8 4.7 %collective-permute-start.6 = (f32[4,16,384]{2,1,0:T(8,128)S(1)}, f32[4,16,384]{2,1,0:T(8,128)S(1)}, u32[]{:S(2)}, u32[]{:S(2)}) collective-permute-start(f32[4,16,384]{2,1,0:T(8,128)S(1)} %get-tuple-element.31), channel_id=1, source_target_pairs={{1,0},{2,1},{3,2},{4,3},{5,4},{6,5},{7,6},{8,7},{9,8},{10,9},{11,1... | collective-permute-start | bytes 294920 | tf_op jit(solution)/shard_map/ppermute | solution.py:18
  111.3 7.7 %collective-permute-start.7 = (f32[4,16,384]{2,1,0:T(8,128)S(1)}, f32[4,16,384]{2,1,0:T(8,128)S(1)}, u32[]{:S(2)}, u32[]{:S(2)}) collective-permute-start(f32[4,16,384]{2,1,0:T(8,128)S(1)} %get-tuple-element.32), channel_id=1, source_target_pairs={{0,1},{1,2},{2,3},{3,4},{4,5},{5,6},{6,7},{7,8},{8,9},{9,10},{10,1... | collective-permute-start | bytes 294920 | tf_op jit(solution)/shard_map/ppermute | solution.py:15
Sparse Core Ops, SparseCore 0:
  134.9 322.1 all-reduce.5
where the time goes:
time: 467 us; the launch traced here: 466 us
  waiting for transfers between devices  328 us (70%)
  other arithmetic  35.3 us (8%)
  local copies, waits for them, and re-layouts  34.5 us (7%)
  blocking collectives  25.4 us (5%)
  starting transfers between devices  22.2 us (5%)
  between operations  20.3 us (4%)
    psum x1, waiting for transfers between devices, shards(): gradient = lax.psum(early_term + late_term, 'shot')  322 us
    psum x1, blocking collectives, shards(): traces = lax.psum(samples, 'dom')  25.4 us
    gather x2, local copies, waits for them, and re-layouts, sample(): picked = field[local, ycells, zcells]  21.1 us
    ppermute x4, starting transfers between devices, with_halo(): lax.ppermute(lax.slice_in_dim(block, 0, width, axis=dim), axis, backward)  14.5 us
    unnamed x5, other arithmetic  12.9 us
    add x4, other arithmetic, laplace_core(): total + weight * (padded[:, R:R + width_y, R + offset:R + offset + width_...  12.4 us
  transfers between devices with their start and end apart: 9, of which 3 were waited for; matrix products, arithmetic and copies ran while one was open for 5% of the time, Pallas kernels for 0%

commit v1 on v0

--- a/solution.py
+++ b/solution.py
@@ -1,10 +1,19 @@
+import functools
 import jax
 import jax.numpy as jnp
 from jax import lax
 from jax.sharding import PartitionSpec as P
+from jax.lax import all_gather
 
 R = 4
 stencil_weights = (-205.0 / 72.0, 8.0 / 5.0, -1.0 / 5.0, 8.0 / 315.0, -1.0 / 560.0)
+
+
+def meet_surface_here(xx, mesh_name):
+    return all_gather(xx, mesh_name).sum(axis=0)
+
+
+prepare_lines = functools.partial(meet_surface_here, mesh_name="shot")
 
 
 def with_halo(block, sides, width):
@@ -109,7 +118,7 @@
     late_term = adj_two * (fwd_three - 2.0 * fwd_two + recent)
     adj_one = advance(adj_two, adj_now, point_grid(shape, rxc, ryc, rzc, resid_two, base))
     early_term = adj_one * (fwd_two - 2.0 * recent + older)
-    gradient = lax.psum(early_term + late_term, "shot")
+    gradient = prepare_lines(early_term + late_term)
     return (fwd_three[None], adj_one[None], gradient)
 
 

time: 467 us -> 467 us (level)
  the two profiles are of different devices: /device:TPU:2 before, /device:TPU:1 now
where the time goes in v1:
time: 467 us; the launch traced here: 466 us
  waiting for transfers between devices  300 us (64%)
  other arithmetic  58.1 us (12%)
  local copies, waits for them, and re-layouts  33.4 us (7%)
  starting transfers between devices  28.1 us (6%)
  blocking collectives  25.7 us (6%)
  between operations  20.2 us (4%)
    all_gather x1, waiting for transfers between devices, meet_surface_here(): return all_gather(xx, mesh_name).sum(axis=0)  299 us
    psum x1, blocking collectives, shards(): traces = lax.psum(samples, 'dom')  25.7 us
    add x4, other arithmetic, laplace_core(): total + weight * (padded[:, R:R + width_y, R + offset:R + offset + width_...  21.6 us
    gather x2, local copies, waits for them, and re-layouts, sample(): picked = field[local, ycells, zcells]  21.1 us
    ppermute x4, starting transfers between devices, with_halo(): lax.ppermute(lax.slice_in_dim(block, 0, width, axis=dim), axis, backward)  17.4 us
    unnamed x5, other arithmetic  14.2 us
    ppermute x4, starting transfers between devices, with_halo(): lax.ppermute(lax.slice_in_dim(block, block.shape[dim] - width, None, axis...  10.6 us
    reduce_sum x1, other arithmetic, meet_surface_here(): return all_gather(xx, mesh_name).sum(axis=0)  10.2 us
  transfers between devices with their start and end apart: 9, of which 3 were waited for; matrix products, arithmetic and copies ran while one was open for 8% of the time, Pallas kernels for 0%

profile of v1, /device:TPU:1, one launch (start us, length us, event | category | flops | bytes accessed | tf_op | source)
XLA Modules:
  0.0 466.1 jit_solution(15795087345799210874)
XLA Ops:
  7.2 1.7 slice_bitcast_fusion.1
  9.0 8.8 %collective-permute-start.4 = (f32[4,16,384]{2,1,0:T(8,128)}, f32[4,16,384]{2,1,0:T(8,128)S(1)}, u32[]{:S(2)}, u32[]{:S(2)}) collective-permute-start(f32[4,16,384]{2,1,0:T(8,128)} %get-tuple-element.33), channel_id=1, source_target_pairs={{1,0},{2,1},{3,2},{4,3},{5,4},{6,5},{7,6},{8,7},{9,8},{10,9},{11,1... | collective-permute-start | bytes 294920 | tf_op jit(solution)/shard_map/ppermute | solution.py:27
  17.7 1.9 collective-permute-start.5
  20.6 2.4 collective-permute-start
  23.0 3.2 collective-permute-start.1
  37.8 12.0 %fusion.80 = f32[32,16,384]{2,1,0:T(8,128)S(1)} fusion(f32[32,16,384]{2,1,0:T(8,128)} %bitcast.68, f32[4,16,384]{2,1,0:T(8,128)S(1)} %collective-permute-done.1, f32[4,16,384]{2,1,0:T(8,128)S(1)} %collective-permute-done), kind=kLoop, calls=%fused_computation.196 | loop fusion | flops 8847360 | bytes 1769472 | tf_op jit(solution)/shard_map/add | solution.py:48
  51.2 1.4 fusion.169
  53.3 1.9 collective-permute-start.2
  55.3 3.6 collective-permute-start.3
  58.9 2.7 fusion.32
  61.7 10.6 %gather_fusion = f32[1024]{0:T(1024)S(1)} fusion(f32[32,16,384]{2,1,0:T(8,128)S(1)} %fusion.169, s32[1024]{0:T(1024)S(1)} %bitcast.64), kind=kCustom, calls=%fused_computation | custom fusion | bytes 20480 | tf_op jit(solution)/shard_map/gather | solution.py:67
  72.3 3.5 fusion.56
  79.1 1.6 multiply_add_fusion.1
  80.7 10.6 %gather_fusion.1 = f32[1024]{0:T(1024)S(1)} fusion(f32[32,16,384]{2,1,0:T(8,128)S(1)} %multiply_add_fusion.1, s32[1024]{0:T(1024)S(1)} %bitcast.65), kind=kCustom, calls=%fused_computation.1 | custom fusion | bytes 20480 | tf_op jit(solution)/shard_map/gather | solution.py:67
  91.3 25.7 %psum.7 = f32[2,1024]{1,0:T(2,128)S(1)} all-reduce(f32[2,1024]{1,0:T(2,128)S(1)} %pad_maximum_fusion.8), channel_id=1, replica_groups=mesh['shot'=32,'dom'=16] {'dom'}, use_global_device_ids=true, to_apply=%region_1.2 | all-reduce | flops 2048 | bytes 16384 | tf_op jit(solution)/shard_map/psum | solution.py:114
  117.1 6.4 %scatter_fusion = f32[196608]{0:T(1024)S(1)} fusion(f32[196608]{0:T(1024)S(1)} %reshape.178, s32[1024]{0:T(1024)S(1)} %broadcast_select_fusion, f32[1024]{0:T(1024)S(1)} %get-tuple-element.48), kind=kCustom, calls=%fused_computation.2 | custom fusion | flops 1024 | bytes 16384
  124.5 2.0 fusion.168
  126.6 4.3 collective-permute-start.6
  130.9 1.9 collective-permute-start.7
  134.5 3.4 fusion.8
  139.1 6.4 %scatter_fusion.1 = f32[196608]{0:T(1024)S(1)} fusion(f32[196608]{0:T(1024)S(1)} %reshape.182, s32[1024]{0:T(1024)S(1)} %broadcast_select_fusion, f32[1024]{0:T(1024)S(1)} %get-tuple-element.47), kind=kCustom, calls=%fused_computation.3 | custom fusion | flops 1024 | bytes 16384
  146.6 3.6 fusion.171
  150.2 298.8 %all-gather.3.cloned.1.call-done = f32[1024,16,384]{2,1,0:T(8,128)} async-done(((f32[32,16,384]{2,1,0:T(8,128)}), f32[1024,16,384]{2,1,0:T(8,128)}) %all-gather.3.cloned.1.call-update) | async-done | bytes 25165840 | tf_op jit(solution)/shard_map/all_gather | solution.py:13
  449.0 10.2 %reduce_sum.9 = f32[32,16,384]{2,1,0:T(8,128)} reduce(f32[32,32,16,384]{3,2,1,0:T(8,128)} %bitcast.67, f32[]{:T(128)} %constant.68.clone.1), dimensions={0}, to_apply=%region_4.5 | reduce | flops 6094848 | bytes 25952260 | tf_op jit(solution)/shard_map/reduce_sum | solution.py:13
  (47 shorter events, 17.2 us)
Async XLA Ops:
  7.2 44.0 %copy-start.1 = (f32[1,32,16,384]{3,2,1,0:T(8,128)S(1)}, f32[1,32,16,384]{3,2,1,0:T(8,128)}, u32[]{:S(2)}) copy-start(f32[1,32,16,384]{3,2,1,0:T(8,128)} %param.19) | copy-start | bytes 2359300
  7.2 44.0 %copy-start.2 = (f32[32,16,384]{2,1,0:T(8,128)S(1)}, f32[32,16,384]{2,1,0:T(8,128)}, u32[]{:S(2)}) copy-start(f32[32,16,384]{2,1,0:T(8,128)} %param.17) | copy-start | bytes 2359300
  7.2 441.8 %all-gather.3.cloned.1.call-start = ((), (), s32[]{:S(2)}) async-start(), calls=%async_computation | async-start | bytes 25952256 | tf_op jit(solution)/shard_map/all_gather | solution.py:13
  9.0 49.9 %collective-permute-start.4 = (f32[4,16,384]{2,1,0:T(8,128)}, f32[4,16,384]{2,1,0:T(8,128)S(1)}, u32[]{:S(2)}, u32[]{:S(2)}) collective-permute-start(f32[4,16,384]{2,1,0:T(8,128)} %get-tuple-element.33), channel_id=1, source_target_pairs={{1,0},{2,1},{3,2},{4,3},{5,4},{6,5},{7,6},{8,7},{9,8},{10,9},{11,1... | collective-permute-start | bytes 294920 | tf_op jit(solution)/shard_map/ppermute | solution.py:27
  17.7 41.2 %collective-permute-start.5 = (f32[4,16,384]{2,1,0:T(8,128)}, f32[4,16,384]{2,1,0:T(8,128)S(1)}, u32[]{:S(2)}, u32[]{:S(2)}) collective-permute-start(f32[4,16,384]{2,1,0:T(8,128)} %get-tuple-element.34), channel_id=1, source_target_pairs={{0,1},{1,2},{2,3},{3,4},{4,5},{5,6},{6,7},{7,8},{8,9},{9,10},{10,1... | collective-permute-start | bytes 294920 | tf_op jit(solution)/shard_map/ppermute | solution.py:24
  20.6 17.2 %collective-permute-start = (f32[4,16,384]{2,1,0:T(8,128)S(1)}, f32[4,16,384]{2,1,0:T(8,128)S(1)}, u32[]{:S(2)}, u32[]{:S(2)}) collective-permute-start(f32[4,16,384]{2,1,0:T(8,128)S(1)} %get-tuple-element.37), channel_id=1, source_target_pairs={{1,0},{2,1},{3,2},{4,3},{5,4},{6,5},{7,6},{8,7},{9,8},{10,9},{11,1... | collective-permute-start | bytes 294920 | tf_op jit(solution)/shard_map/ppermute | solution.py:27
  23.0 14.8 %collective-permute-start.1 = (f32[4,16,384]{2,1,0:T(8,128)S(1)}, f32[4,16,384]{2,1,0:T(8,128)S(1)}, u32[]{:S(2)}, u32[]{:S(2)}) collective-permute-start(f32[4,16,384]{2,1,0:T(8,128)S(1)} %get-tuple-element.38), channel_id=1, source_target_pairs={{0,1},{1,2},{2,3},{3,4},{4,5},{5,6},{6,7},{7,8},{8,9},{9,10},{10,1... | collective-permute-start | bytes 294920 | tf_op jit(solution)/shard_map/ppermute | solution.py:24
  51.2 7.7 %copy-start.3 = (f32[1,32,16,384]{3,2,1,0:T(8,128)S(1)}, f32[1,32,16,384]{3,2,1,0:T(8,128)}, u32[]{:S(2)}) copy-start(f32[1,32,16,384]{3,2,1,0:T(8,128)} %param.21) | copy-start | bytes 2359300
  53.3 19.0 %collective-permute-start.2 = (f32[4,16,384]{2,1,0:T(8,128)}, f32[4,16,384]{2,1,0:T(8,128)S(1)}, u32[]{:S(2)}, u32[]{:S(2)}) collective-permute-start(f32[4,16,384]{2,1,0:T(8,128)} %get-tuple-element.35), channel_id=1, source_target_pairs={{1,0},{2,1},{3,2},{4,3},{5,4},{6,5},{7,6},{8,7},{9,8},{10,9},{11,1... | collective-permute-start | bytes 294920 | tf_op jit(solution)/shard_map/ppermute | solution.py:27
  55.3 17.1 %collective-permute-start.3 = (f32[4,16,384]{2,1,0:T(8,128)}, f32[4,16,384]{2,1,0:T(8,128)S(1)}, u32[]{:S(2)}, u32[]{:S(2)}) collective-permute-start(f32[4,16,384]{2,1,0:T(8,128)} %get-tuple-element.36), channel_id=1, source_target_pairs={{0,1},{1,2},{2,3},{3,4},{4,5},{5,6},{6,7},{7,8},{8,9},{9,10},{10,1... | collective-permute-start | bytes 294920 | tf_op jit(solution)/shard_map/ppermute | solution.py:24
  80.7 65.9 %copy-start = (f32[32,16,384]{2,1,0:T(8,128)}, f32[32,16,384]{2,1,0:T(8,128)S(1)}, u32[]{:S(2)}) copy-start(f32[32,16,384]{2,1,0:T(8,128)S(1)} %multiply_add_fusion.1) | copy-start | bytes 2359300
  80.7 10.6 %copy-start.5 = (s32[1,1024]{1,0:T(1,128)S(1)}, s32[1,1024]{1,0:T(1,128)}, u32[]{:S(2)}) copy-start(s32[1,1024]{1,0:T(1,128)} %param.26) | copy-start | bytes 12292
  80.7 36.4 %copy-start.6 = (pred[1024]{0:T(1024)(128)(4,1)S(1)}, pred[1024]{0:T(1024)(128)(4,1)}, u32[]{:S(2)}) copy-start(pred[1024]{0:T(1024)(128)(4,1)} %fusion.172) | copy-start | bytes 3076
  126.6 7.9 %copy-start.4 = (f32[32,16,384]{2,1,0:T(8,128)}, f32[32,16,384]{2,1,0:T(8,128)S(1)}, u32[]{:S(2)}) copy-start(f32[32,16,384]{2,1,0:T(8,128)S(1)} %fusion.168) | copy-start | bytes 2359300
  126.6 6.8 %collective-permute-start.6 = (f32[4,16,384]{2,1,0:T(8,128)S(1)}, f32[4,16,384]{2,1,0:T(8,128)S(1)}, u32[]{:S(2)}, u32[]{:S(2)}) collective-permute-start(f32[4,16,384]{2,1,0:T(8,128)S(1)} %get-tuple-element.31), channel_id=1, source_target_pairs={{1,0},{2,1},{3,2},{4,3},{5,4},{6,5},{7,6},{8,7},{9,8},{10,9},{11,1... | collective-permute-start | bytes 294920 | tf_op jit(solution)/shard_map/ppermute | solution.py:27
  130.9 3.5 collective-permute-start.7
Sparse Core Ops, SparseCore 0:
  150.3 298.6 all-gather.2
